TPU v7x, 512 devices: a whole 4x4x16 slice. The times are simulated.
512 devices in a mesh: context: 128 (over z, y, core), tensor: 4 (over x).
Axes of the slice: x: 4, y: 4, z: 16, core: 2. Of those that a mesh axis runs over, the one named last changes fastest.
Arguments:
- projected: bfloat16 [3, 16, 512, 16384], P(None, 'tensor', None, 'context'), may hold values from -6 to 6
- long_filter: bfloat16 [512, 128], replicated, may hold values from -0.5 to 0.5
- cotangent: bfloat16 [16, 512, 16384], P('tensor', None, 'context'), may hold values from -6 to 6
Outputs:
- mixed: bfloat16 [16, 512, 16384], P('tensor', None, 'context')
- stream_grads: bfloat16 [3, 16, 512, 16384], P(None, 'tensor', None, 'context')
- filter_grads: float32 [512, 128], P('context')
All inputs are finite; a program needn't handle non-finite values.
Results may differ from a plain program's by a relative error of at most 0.0057.
Values may be sent and summed in bfloat16 or wider, within the bound.
No kernel may reach another device: no remote copies, remote signals or barrier semaphores. Data moves between devices by JAX's collectives and lax.ppermute only.
A program may use at most 64 MiB of HBM per device.

v0:
```python
import math

import jax
import jax.numpy as jnp
from jax import lax
from jax.sharding import PartitionSpec as P

CONTEXT = ("z", "y", "core")


def grouped_conv(lhs, rhs, groups):
    return lax.conv_general_dilated(
        lhs,
        rhs,
        window_strides=(1,),
        padding="VALID",
        dimension_numbers=("NCH", "OIH", "NCH"),
        feature_group_count=groups,
        preferred_element_type=jnp.float32,
    )


def halving_step(rows, axis, bit, cover=None):
    size = lax.axis_size(axis)
    index = lax.axis_index(axis)
    split = rows.reshape((rows.shape[0] // 2, 2) + rows.shape[1:])
    upper = ((index >> bit) & 1) == 1
    keep = jnp.where(upper, split[:, 1], split[:, 0])
    give = jnp.where(upper, split[:, 0], split[:, 1])
    pairs = [(i, i ^ (1 << bit)) for i in range(size)]
    if cover is None:
        return keep + lax.ppermute(give, axis, pairs)
    work, operands = cover
    give, operands = lax.optimization_barrier((give, operands))
    received = lax.ppermute(give, axis, pairs)
    received, done = lax.optimization_barrier((received, work(*operands)))
    return (keep + received, done)


def butterfly_sum(values, axis):
    size = lax.axis_size(axis)
    bit = 0
    while (1 << bit) < size:
        pairs = [(i, i ^ (1 << bit)) for i in range(size)]
        values = values + lax.ppermute(values, axis, pairs)
        bit += 1
    return values


def body(projected, long_filter, cotangent):
    filter_taps = long_filter.shape[1]
    query_stream = projected[0]
    key_stream = projected[1]
    value_stream = projected[2]
    members, groups, local_tokens = key_stream.shape
    blocks = lax.axis_size(CONTEXT)
    length = local_tokens * blocks
    factor = 1.0 / math.sqrt(members * lax.axis_size("tensor") * length)
    gated = (key_stream.astype(jnp.float32) * value_stream.astype(jnp.float32)).astype(jnp.bfloat16)
    grad_filtered = (cotangent.astype(jnp.float32) * query_stream.astype(jnp.float32)).astype(
        jnp.bfloat16
    )
    earlier = lax.ppermute(gated, CONTEXT, [(i, i + 1) for i in range(blocks - 1)])
    later = lax.ppermute(grad_filtered, CONTEXT, [(i + 1, i) for i in range(blocks - 1)])
    halo = filter_taps - 1
    gated_ext = jnp.concatenate([earlier[:, :, local_tokens - halo:], gated], 2)
    grad_ext = jnp.concatenate([grad_filtered, later[:, :, :halo]], 2)
    reversed_taps = long_filter[:, ::-1][:, None, :]
    tap_sums = lax.conv_general_dilated(
        gated_ext,
        grad_filtered,
        window_strides=(1,),
        padding=((0, 0),),
        dimension_numbers=lax.ConvDimensionNumbers((1, 0, 2), (1, 0, 2), (1, 0, 2)),
        batch_group_count=groups,
        preferred_element_type=jnp.float32,
    )
    partial_taps = tap_sums[:, 0, ::-1]
    rows = partial_taps.reshape(blocks, groups // blocks, filter_taps)
    forward = lambda lhs, rhs: grouped_conv(lhs, rhs, groups).astype(jnp.bfloat16)
    rows = halving_step(rows, "core", 0)
    rows, filtered = halving_step(rows, "y", 0, (forward, (gated_ext, reversed_taps)))
    rows, grad_gated = halving_step(rows, "y", 1, (forward, (grad_ext, long_filter[:, None, :])))
    rows = lax.all_to_all(rows, "z", split_axis=0, concat_axis=0, tiled=True)
    own_taps = jnp.sum(rows, axis=0, keepdims=True)
    filter_grads = butterfly_sum(own_taps[0], "tensor") * factor
    filtered_wide = filtered.astype(jnp.float32)
    grad_wide = grad_gated.astype(jnp.float32)
    mixed = (query_stream.astype(jnp.float32) * filtered_wide).astype(jnp.bfloat16)
    stream_grads = jnp.stack(
        [
            cotangent.astype(jnp.float32) * filtered_wide,
            grad_wide * value_stream.astype(jnp.float32),
            grad_wide * key_stream.astype(jnp.float32),
        ]
    ).astype(jnp.bfloat16)
    return (mixed, stream_grads, filter_grads)


def solution(mesh):
    contexts, tensors = mesh.devices.shape
    split = mesh.devices.reshape(contexts // 8, 4, 2, tensors)
    fine = jax.sharding.Mesh(split, CONTEXT + ("tensor",))
    in_specs = (P(None, "tensor", None, CONTEXT), P(), P("tensor", None, CONTEXT))
    out_specs = (
        P("tensor", None, CONTEXT),
        P(None, "tensor", None, CONTEXT),
        P(CONTEXT, None),
    )
    return jax.shard_map(body, mesh=fine, in_specs=in_specs, out_specs=out_specs, check_vma=False)
```

profile of v0, /device:TPU:24, one launch (start us, length us, event | category | flops | bytes accessed | tf_op | source)
XLA Modules:
  0.0 119.9 jit_solution(13815456356553846460)
XLA Ops:
  0.6 1.5 %fusion.14 = (bf16[1,4,512,128]{3,2,1,0:T(8,128)(2,1)S(1)}, bf16[1,4,512,128]{3,2,1,0:T(8,128)(2,1)S(1)}, bf16[1,4,512,128]{3,2,1,0:T(8,128)(2,1)S(1)}) fusion(bf16[3,4,512,128]{3,2,1,0:T(8,128)(2,1)} %param.3), kind=kLoop, calls=%fused_computation.32 | loop fusion | bytes 3145728 | tf_op jit(solution)/shard_map/slice | solution.py:54
  2.1 0.4 copy.48
  2.5 0.4 copy.49
  3.2 1.9 %collective-permute-start = (bf16[4,512,128]{1,0,2:T(4,128)(2,1)S(1)}, bf16[4,512,128]{1,0,2:T(4,128)(2,1)}, u32[]{:S(2)}, u32[]{:S(2)}) collective-permute-start(bf16[4,512,128]{1,0,2:T(4,128)(2,1)S(1)} %fusion.4), channel_id=1, source_target_pairs={{0,4},{4,8},{8,12},{12,16},{16,20},{20,24},{24,28},{28,32},{32,36}... | collective-permute-start | bytes 1572872 | tf_op jit(solution)/shard_map/ppermute | solution.py:63
  5.1 0.4 copy.47
  5.6 1.6 %copy.29 = bf16[4,512,128]{1,0,2:T(4,128)(2,1)S(1)} copy(bf16[4,512,128]{2,1,0:T(8,128)(2,1)} %param.5) | data formatting | bytes 1048576 | tf_op args[2]
  7.2 0.3 fusion.1
  7.5 3.6 %collective-permute-start.3 = (bf16[4,512,128]{1,0,2:T(4,128)(2,1)S(1)}, bf16[4,512,128]{1,0,2:T(4,128)(2,1)}, u32[]{:S(2)}, u32[]{:S(2)}) collective-permute-start(bf16[4,512,128]{1,0,2:T(4,128)(2,1)S(1)} %fusion.1), channel_id=1, source_target_pairs={{4,0},{8,4},{12,8},{16,12},{20,16},{24,20},{28,24},{32,28},{36,32}... | collective-permute-start | bytes 1572872 | tf_op jit(solution)/shard_map/ppermute | solution.py:64
  11.2 0.6 rev.7
  11.8 2.0 %collective-permute-done = bf16[4,512,128]{1,0,2:T(4,128)(2,1)} collective-permute-done((bf16[4,512,128]{1,0,2:T(4,128)(2,1)S(1)}, bf16[4,512,128]{1,0,2:T(4,128)(2,1)}, u32[]{:S(2)}, u32[]{:S(2)}) %collective-permute-start) | collective-permute-done | bytes 524320 | tf_op jit(solution)/shard_map/ppermute | solution.py:63
  13.8 1.2 %slice.50 = bf16[4,512,127]{1,0,2:T(4,128)(2,1)S(1)} slice(bf16[4,512,128]{1,0,2:T(4,128)(2,1)} %collective-permute-done), slice={[0:4], [0:512], [1:128]} | slice | bytes 1040384 | tf_op jit(solution)/shard_map/slice | solution.py:66
  15.0 23.5 %fusion.13 = f32[512,1,128]{0,1,2:T(1,128)S(1)} fusion(bf16[4,512,128]{1,0,2:T(4,128)(2,1)S(1)} %fusion.1, bf16[4,512,128]{1,0,2:T(4,128)(2,1)S(1)} %fusion.4, bf16[4,512,127]{1,0,2:T(4,128)(2,1)S(1)} %slice.50), kind=kOutput, calls=%fused_computation.31 | convolution fusion | flops 69197824 | bytes 1830912 | tf_op jit(solution)/shard_map/conv_general_dilated | solution.py:69
  38.8 1.9 %collective-permute-start.1 = (f32[64,4,128]{2,1,0:T(4,128)S(1)}, f32[64,4,128]{2,1,0:T(4,128)S(1)}, u32[]{:S(2)}, u32[]{:S(2)}) collective-permute-start(f32[64,4,128]{2,1,0:T(4,128)S(1)} %select_bitcast_fusion), channel_id=1, source_target_pairs={{0,4},{4,0},{1,5},{5,1},{2,6},{6,2},{3,7},{7,3},{8,12},{12,8},{9,1... | collective-permute-start | bytes 393224 | tf_op jit(solution)/shard_map/ppermute | solution.py:32
  40.8 0.7 pad_maximum_fusion.1
  41.5 1.2 %slice.57 = bf16[4,512,127]{1,0,2:T(4,128)(2,1)S(1)} slice(bf16[4,512,128]{1,0,2:T(4,128)(2,1)} %collective-permute-done.3), slice={[0:4], [0:512], [0:127]} | slice | bytes 1040384 | tf_op jit(solution)/shard_map/slice | solution.py:67
  42.7 1.6 %pad_maximum_fusion.2 = bf16[4,512,255]{1,0,2:T(4,128)(2,1)} fusion(bf16[4,512,127]{1,0,2:T(4,128)(2,1)S(1)} %slice.57, bf16[4,512,128]{1,0,2:T(4,128)(2,1)S(1)} %fusion.1), kind=kLoop, calls=%fused_computation.16 | loop fusion | flops 522240 | bytes 2088960 | tf_op jit(solution)/shard_map/concatenate | solution.py:67
  44.6 2.8 %collective-permute-start.2 = (f32[32,4,128]{2,1,0:T(4,128)S(1)}, f32[32,4,128]{2,1,0:T(4,128)S(1)}, u32[]{:S(2)}, u32[]{:S(2)}) collective-permute-start(f32[32,4,128]{2,1,0:T(4,128)S(1)} %fusion.11), channel_id=1, source_target_pairs={{0,8},{8,0},{16,24},{24,16},{1,9},{9,1},{17,25},{25,17},{2,10},{10... | collective-permute-start | bytes 196616 | tf_op jit(solution)/shard_map/ppermute | solution.py:35
  47.4 11.2 %convolution_convert_fusion.1 = bf16[4,512,128]{1,0,2:T(4,128)(2,1)} fusion(bf16[4,512,255]{1,0,2:T(4,128)(2,1)S(1)} %pad_maximum_fusion.1, bf16[512,1,128]{0,1,2:T(2,128)(2,1)S(1)} %copy.37), kind=kOutput, calls=%fused_computation.8 | convolution fusion | flops 67371008 | bytes 1699840 | tf_op jit(solution)/shard_map/conv_general_dilated | solution.py:12
  58.9 5.3 %collective-permute-start.4 = (f32[16,4,128]{2,1,0:T(4,128)S(1)}, f32[16,4,128]{2,1,0:T(4,128)S(1)}, u32[]{:S(2)}, u32[]{:S(2)}) collective-permute-start(f32[16,4,128]{2,1,0:T(4,128)S(1)} %fusion.12), channel_id=1, source_target_pairs={{0,16},{8,24},{16,0},{24,8},{1,17},{9,25},{17,1},{25,9},{2,18},{10... | collective-permute-start | bytes 98312 | tf_op jit(solution)/shard_map/ppermute | solution.py:35
  64.2 11.5 %convolution_convert_fusion = bf16[4,512,128]{1,0,2:T(4,128)(2,1)} fusion(bf16[4,512,255]{1,0,2:T(4,128)(2,1)S(1)} %copy-done.8, bf16[512,1,128]{0,1,2:T(2,128)(2,1)S(1)} %copy.42), kind=kOutput, calls=%fused_computation.7 | convolution fusion | flops 67371008 | bytes 1699840 | tf_op jit(solution)/shard_map/conv_general_dilated | solution.py:12
  75.7 0.6 bitcast_add_fusion.1
  76.3 16.2 %all-to-all-start = ((f32[16,4,128]{2,1,0:T(4,128)}), f32[16,4,128]{2,1,0:T(4,128)S(1)}, u32[]{:S(2)}, u32[]{:S(2)}) async-start(f32[16,4,128]{2,1,0:T(4,128)} %bitcast_add_fusion.1), calls=%async_computation | async-start | bytes 65536 | tf_op jit(solution)/shard_map/all_to_all | solution.py:84
  92.6 1.7 %fusion.8 = (bf16[1,4,512,128]{2,1,3,0:T(4,128)(2,1)S(1)}, bf16[4,512,128]{1,0,2:T(4,128)(2,1)S(1)}) fusion(bf16[4,512,128]{1,0,2:T(4,128)(2,1)} %convolution_convert_fusion.1, bf16[4,512,128]{1,0,2:T(4,128)(2,1)S(1)} %copy-done.7, bf16[1,4,512,128]{2,1,3,0:T(4,128)(2,1)S(1)} %copy-done.5), kind=kLoop, calls=%fused_computation.19 | loop fusion | flops 1835008 | bytes 2621440 | tf_op jit(solution)/shard_map/stack | solution.py:90
  94.3 1.2 copy.45
  95.5 9.6 %all-to-all-done = f32[16,4,128]{2,1,0:T(4,128)S(1)} async-done(((f32[16,4,128]{2,1,0:T(4,128)}), f32[16,4,128]{2,1,0:T(4,128)S(1)}, u32[]{:S(2)}, u32[]{:S(2)}) %all-to-all-start) | async-done | bytes 32800 | tf_op jit(solution)/shard_map/all_to_all | solution.py:84
  105.2 3.4 %collective-permute-start.5 = (f32[4,128]{1,0:T(4,128)S(1)}, f32[4,128]{1,0:T(4,128)S(1)}, u32[]{:S(2)}, u32[]{:S(2)}) collective-permute-start(f32[4,128]{1,0:T(4,128)S(1)} %reduce_sum.9), channel_id=1, source_target_pairs={{0,1},{1,0},{2,3},{3,2},{4,5},{5,4},{6,7},{7,6},{8,9},{9,8},{10,11... | collective-permute-start | bytes 6152 | tf_op jit(solution)/shard_map/ppermute | solution.py:45
  108.6 1.6 %fusion.7 = (bf16[1,4,512,128]{2,1,3,0:T(4,128)(2,1)S(1)}, bf16[1,4,512,128]{2,1,3,0:T(4,128)(2,1)S(1)}) fusion(bf16[4,512,128]{1,0,2:T(4,128)(2,1)} %convolution_convert_fusion, bf16[1,4,512,128]{2,1,3,0:T(4,128)(2,1)S(1)} %copy-done.3, bf16[1,4,512,128]{2,1,3,0:T(4,128)(2,1)S(1)} %copy-done.1), kind=kLoop, calls=%fused_computation.18 | loop fusion | flops 1835008 | bytes 2621440 | tf_op jit(solution)/shard_map/stack | solution.py:90
  110.2 0.5 collective-permute-done.5
  110.6 4.9 %collective-permute-start.6 = (f32[4,128]{1,0:T(4,128)S(1)}, f32[4,128]{1,0:T(4,128)S(1)}, u32[]{:S(2)}, u32[]{:S(2)}) collective-permute-start(f32[4,128]{1,0:T(4,128)S(1)} %add.18), channel_id=1, source_target_pairs={{0,2},{1,3},{2,0},{3,1},{4,6},{5,7},{6,4},{7,5},{8,10},{9,11},{10,... | collective-permute-start | bytes 6152 | tf_op jit(solution)/shard_map/ppermute | solution.py:45
  115.6 1.3 %pad_maximum_fusion = bf16[3,4,512,128]{2,1,3,0:T(4,128)(2,1)S(1)} fusion(bf16[1,4,512,128]{2,1,3,0:T(4,128)(2,1)S(1)} %get-tuple-element.35, bf16[1,4,512,128]{2,1,3,0:T(4,128)(2,1)S(1)} %get-tuple-element.34, bf16[1,4,512,128]{2,1,3,0:T(4,128)(2,1)S(1)} %get-tuple-element.32), kind=kLoop, calls=%fused_computation | loop fusion | flops 1572864 | bytes 3145728 | tf_op jit(solution)/shard_map/stack | solution.py:90
  116.9 2.5 %copy.46 = bf16[3,4,512,128]{3,2,1,0:T(8,128)(2,1)} copy(bf16[3,4,512,128]{2,1,3,0:T(4,128)(2,1)S(1)} %pad_maximum_fusion) | data formatting | bytes 3145728
  119.4 0.6 add_multiply_fusion
  (37 shorter events, 1.1 us)
Async XLA Ops:
  2.5 3.0 %copy-start = (bf16[1,4,512,128]{2,1,3,0:T(4,128)(2,1)}, bf16[1,4,512,128]{2,1,3,0:T(4,128)(2,1)S(1)}, u32[]{:S(2)}) copy-start(bf16[1,4,512,128]{2,1,3,0:T(4,128)(2,1)S(1)} %copy.48) | copy-start | bytes 1572868
  2.9 4.3 %copy-start.2 = (bf16[1,4,512,128]{2,1,3,0:T(4,128)(2,1)}, bf16[1,4,512,128]{2,1,3,0:T(4,128)(2,1)S(1)}, u32[]{:S(2)}) copy-start(bf16[1,4,512,128]{2,1,3,0:T(4,128)(2,1)S(1)} %copy.49) | copy-start | bytes 1572868
  3.2 10.6 %collective-permute-start = (bf16[4,512,128]{1,0,2:T(4,128)(2,1)S(1)}, bf16[4,512,128]{1,0,2:T(4,128)(2,1)}, u32[]{:S(2)}, u32[]{:S(2)}) collective-permute-start(bf16[4,512,128]{1,0,2:T(4,128)(2,1)S(1)} %fusion.4), channel_id=1, source_target_pairs={{0,4},{4,8},{8,12},{12,16},{16,20},{20,24},{24,28},{28,32},{32,36}... | collective-permute-start | bytes 1572872 | tf_op jit(solution)/shard_map/ppermute | solution.py:63
  5.6 9.5 %copy-start.4 = (bf16[1,4,512,128]{2,1,3,0:T(4,128)(2,1)}, bf16[1,4,512,128]{2,1,3,0:T(4,128)(2,1)S(1)}, u32[]{:S(2)}) copy-start(bf16[1,4,512,128]{2,1,3,0:T(4,128)(2,1)S(1)} %copy.47) | copy-start | bytes 1572868
  5.6 5.6 %copy-start.9 = (bf16[512,128]{1,0:T(8,128)(2,1)S(1)}, bf16[512,128]{1,0:T(8,128)(2,1)}, u32[]{:S(2)}) copy-start(bf16[512,128]{1,0:T(8,128)(2,1)} %param.4) | copy-start | bytes 393220
  7.2 31.4 %copy-start.6 = (bf16[4,512,128]{1,0,2:T(4,128)(2,1)}, bf16[4,512,128]{1,0,2:T(4,128)(2,1)S(1)}, u32[]{:S(2)}) copy-start(bf16[4,512,128]{1,0,2:T(4,128)(2,1)S(1)} %copy.29) | copy-start | bytes 1572868
  7.5 33.9 %collective-permute-start.3 = (bf16[4,512,128]{1,0,2:T(4,128)(2,1)S(1)}, bf16[4,512,128]{1,0,2:T(4,128)(2,1)}, u32[]{:S(2)}, u32[]{:S(2)}) collective-permute-start(bf16[4,512,128]{1,0,2:T(4,128)(2,1)S(1)} %fusion.1), channel_id=1, source_target_pairs={{4,0},{8,4},{12,8},{16,12},{20,16},{24,20},{28,24},{32,28},{36,32}... | collective-permute-start | bytes 1572872 | tf_op jit(solution)/shard_map/ppermute | solution.py:64
  38.8 5.5 %collective-permute-start.1 = (f32[64,4,128]{2,1,0:T(4,128)S(1)}, f32[64,4,128]{2,1,0:T(4,128)S(1)}, u32[]{:S(2)}, u32[]{:S(2)}) collective-permute-start(f32[64,4,128]{2,1,0:T(4,128)S(1)} %select_bitcast_fusion), channel_id=1, source_target_pairs={{0,4},{4,0},{1,5},{5,1},{2,6},{6,2},{3,7},{7,3},{8,12},{12,8},{9,1... | collective-permute-start | bytes 393224 | tf_op jit(solution)/shard_map/ppermute | solution.py:32
  44.6 19.6 %copy-start.8 = (bf16[4,512,255]{1,0,2:T(4,128)(2,1)S(1)}, bf16[4,512,255]{1,0,2:T(4,128)(2,1)}, u32[]{:S(2)}) copy-start(bf16[4,512,255]{1,0,2:T(4,128)(2,1)} %pad_maximum_fusion.2) | copy-start | bytes 3133444
  44.6 14.0 %collective-permute-start.2 = (f32[32,4,128]{2,1,0:T(4,128)S(1)}, f32[32,4,128]{2,1,0:T(4,128)S(1)}, u32[]{:S(2)}, u32[]{:S(2)}) collective-permute-start(f32[32,4,128]{2,1,0:T(4,128)S(1)} %fusion.11), channel_id=1, source_target_pairs={{0,8},{8,0},{16,24},{24,16},{1,9},{9,1},{17,25},{25,17},{2,10},{10... | collective-permute-start | bytes 196616 | tf_op jit(solution)/shard_map/ppermute | solution.py:35
  58.9 33.7 %copy-start.5 = (bf16[1,4,512,128]{2,1,3,0:T(4,128)(2,1)S(1)}, bf16[1,4,512,128]{2,1,3,0:T(4,128)(2,1)}, u32[]{:S(2)}) copy-start(bf16[1,4,512,128]{2,1,3,0:T(4,128)(2,1)} %copy-done.4) | copy-start | bytes 1572868
  58.9 33.7 %copy-start.7 = (bf16[4,512,128]{1,0,2:T(4,128)(2,1)S(1)}, bf16[4,512,128]{1,0,2:T(4,128)(2,1)}, u32[]{:S(2)}) copy-start(bf16[4,512,128]{1,0,2:T(4,128)(2,1)} %copy-done.6) | copy-start | bytes 1572868
  58.9 16.8 %collective-permute-start.4 = (f32[16,4,128]{2,1,0:T(4,128)S(1)}, f32[16,4,128]{2,1,0:T(4,128)S(1)}, u32[]{:S(2)}, u32[]{:S(2)}) collective-permute-start(f32[16,4,128]{2,1,0:T(4,128)S(1)} %fusion.12), channel_id=1, source_target_pairs={{0,16},{8,24},{16,0},{24,8},{1,17},{9,25},{17,1},{25,9},{2,18},{10... | collective-permute-start | bytes 98312 | tf_op jit(solution)/shard_map/ppermute | solution.py:35
  76.3 28.8 %all-to-all-start = ((f32[16,4,128]{2,1,0:T(4,128)}), f32[16,4,128]{2,1,0:T(4,128)S(1)}, u32[]{:S(2)}, u32[]{:S(2)}) async-start(f32[16,4,128]{2,1,0:T(4,128)} %bitcast_add_fusion.1), calls=%async_computation | async-start | bytes 65536 | tf_op jit(solution)/shard_map/all_to_all | solution.py:84
  92.6 16.0 %copy-start.1 = (bf16[1,4,512,128]{2,1,3,0:T(4,128)(2,1)S(1)}, bf16[1,4,512,128]{2,1,3,0:T(4,128)(2,1)}, u32[]{:S(2)}) copy-start(bf16[1,4,512,128]{2,1,3,0:T(4,128)(2,1)} %copy-done) | copy-start | bytes 1572868
  92.6 16.0 %copy-start.3 = (bf16[1,4,512,128]{2,1,3,0:T(4,128)(2,1)S(1)}, bf16[1,4,512,128]{2,1,3,0:T(4,128)(2,1)}, u32[]{:S(2)}) copy-start(bf16[1,4,512,128]{2,1,3,0:T(4,128)(2,1)} %copy-done.2) | copy-start | bytes 1572868
  105.2 5.5 %collective-permute-start.5 = (f32[4,128]{1,0:T(4,128)S(1)}, f32[4,128]{1,0:T(4,128)S(1)}, u32[]{:S(2)}, u32[]{:S(2)}) collective-permute-start(f32[4,128]{1,0:T(4,128)S(1)} %reduce_sum.9), channel_id=1, source_target_pairs={{0,1},{1,0},{2,3},{3,2},{4,5},{5,4},{6,7},{7,6},{8,9},{9,8},{10,11... | collective-permute-start | bytes 6152 | tf_op jit(solution)/shard_map/ppermute | solution.py:45
  110.6 8.7 %collective-permute-start.6 = (f32[4,128]{1,0:T(4,128)S(1)}, f32[4,128]{1,0:T(4,128)S(1)}, u32[]{:S(2)}, u32[]{:S(2)}) collective-permute-start(f32[4,128]{1,0:T(4,128)S(1)} %add.18), channel_id=1, source_target_pairs={{0,2},{1,3},{2,0},{3,1},{4,6},{5,7},{6,4},{7,5},{8,10},{9,11},{10,... | collective-permute-start | bytes 6152 | tf_op jit(solution)/shard_map/ppermute | solution.py:45
where the time goes:
time: 121 us; the launch traced here: 120 us
  matrix products  46.3 us (38%)
  starting transfers between devices  40.1 us (33%)
  waiting for transfers between devices  12.1 us (10%)
  local copies, waits for them, and re-layouts  11.6 us (10%)
  other arithmetic  8.82 us (7%)
    conv_general_dilated x1, matrix products, body(): lax.conv_general_dilated(gated_ext, grad_filtered, window_strides=(1,), p...  23.5 us
    conv_general_dilated x2, matrix products, grouped_conv(): lax.conv_general_dilated(lhs, rhs, window_strides=(1,), padding='VALID',...  22.8 us
    all_to_all x1, starting transfers between devices, body(): rows = lax.all_to_all(rows, 'z', split_axis=0, concat_axis=0, tiled=True)  16.2 us
    all_to_all x1, waiting for transfers between devices, body(): rows = lax.all_to_all(rows, 'z', split_axis=0, concat_axis=0, tiled=True)  9.65 us
    ppermute x2, starting transfers between devices, butterfly_sum(): values = values + lax.ppermute(values, axis, pairs)  8.31 us
    ppermute x2, starting transfers between devices, halving_step(): received = lax.ppermute(give, axis, pairs)  8.05 us
    unnamed x26, local copies, waits for them, and re-layouts  6.55 us
    another operation x3, other arithmetic, body(): jnp.stack([cotangent.astype(jnp.float32) * filtered_wide, grad_wide * val...  4.57 us
  transfers between devices with their start and end apart: 8, of which 3 were waited for; matrix products, arithmetic and copies ran while one was open for 52% of the time, Pallas kernels for 0%

commit v1 on v0

--- a/solution.py
+++ b/solution.py
@@ -80,8 +80,10 @@
     forward = lambda lhs, rhs: grouped_conv(lhs, rhs, groups).astype(jnp.bfloat16)
     rows = halving_step(rows, "core", 0)
     rows, filtered = halving_step(rows, "y", 0, (forward, (gated_ext, reversed_taps)))
-    rows, grad_gated = halving_step(rows, "y", 1, (forward, (grad_ext, long_filter[:, None, :])))
+    rows = halving_step(rows, "y", 1)
+    rows, operands = lax.optimization_barrier((rows, (grad_ext, long_filter[:, None, :])))
     rows = lax.all_to_all(rows, "z", split_axis=0, concat_axis=0, tiled=True)
+    rows, grad_gated = lax.optimization_barrier((rows, forward(*operands)))
     own_taps = jnp.sum(rows, axis=0, keepdims=True)
     filter_grads = butterfly_sum(own_taps[0], "tensor") * factor
     filtered_wide = filtered.astype(jnp.float32)

time: 121 us -> 113 us (0.934)
  the two profiles are of different devices: /device:TPU:24 before, /device:TPU:8 now
where the time goes in v1:
time: 113 us
  matrix products  45.6 us (40%)
  starting transfers between devices  39.4 us (35%)
  local copies, waits for them, and re-layouts  11.3 us (10%)
  waiting for transfers between devices  7.95 us (7%)
  other arithmetic  7.58 us (7%)
    conv_general_dilated x1, matrix products, body(): lax.conv_general_dilated(gated_ext, grad_filtered, window_strides=(1,), p...  23.5 us
    conv_general_dilated x2, matrix products, grouped_conv(): lax.conv_general_dilated(lhs, rhs, window_strides=(1,), padding='VALID',...  22.1 us
    all_to_all x1, starting transfers between devices, body(): rows = lax.all_to_all(rows, 'z', split_axis=0, concat_axis=0, tiled=True)  16.6 us
    ppermute x2, starting transfers between devices, butterfly_sum(): values = values + lax.ppermute(values, axis, pairs)  8.31 us
    unnamed x22, local copies, waits for them, and re-layouts  5.28 us
    ppermute x2, starting transfers between devices, halving_step(): return keep + lax.ppermute(give, axis, pairs)  4.49 us
    ppermute x1, starting transfers between devices, halving_step(): received = lax.ppermute(give, axis, pairs)  4.29 us
    ppermute x1, starting transfers between devices, body(): lax.ppermute(grad_filtered, CONTEXT, [(i + 1, i) for i in range(blocks -...  3.64 us
  transfers between devices with their start and end apart: 8, of which 4 were waited for; matrix products, arithmetic and copies ran while one was open for 53% of the time, Pallas kernels for 0%

profile of v1, /device:TPU:8, one launch (start us, length us, event | category | flops | bytes accessed | tf_op | source)
XLA Modules:
  0.0 112.8 jit_solution(6698523151219405084)
XLA Ops:
  0.6 1.5 %fusion.15 = (bf16[1,4,512,128]{3,2,1,0:T(8,128)(2,1)S(1)}, bf16[1,4,512,128]{3,2,1,0:T(8,128)(2,1)S(1)}, bf16[1,4,512,128]{3,2,1,0:T(8,128)(2,1)S(1)}) fusion(bf16[3,4,512,128]{3,2,1,0:T(8,128)(2,1)} %param.3), kind=kLoop, calls=%fused_computation.33 | loop fusion | bytes 3145728 | tf_op jit(solution)/shard_map/slice | solution.py:54
  2.1 0.4 copy.48
  2.5 0.4 copy.49
  3.2 2.1 %collective-permute-start = (bf16[4,512,128]{1,0,2:T(4,128)(2,1)S(1)}, bf16[4,512,128]{1,0,2:T(4,128)(2,1)}, u32[]{:S(2)}, u32[]{:S(2)}) collective-permute-start(bf16[4,512,128]{1,0,2:T(4,128)(2,1)S(1)} %fusion.4), channel_id=1, source_target_pairs={{0,4},{4,8},{8,12},{12,16},{16,20},{20,24},{24,28},{28,32},{32,36}... | collective-permute-start | bytes 1572872 | tf_op jit(solution)/shard_map/ppermute | solution.py:63
  5.3 0.4 copy.47
  5.7 0.4 copy.29
  6.4 3.6 %collective-permute-start.4 = (bf16[4,512,128]{1,0,2:T(4,128)(2,1)S(1)}, bf16[4,512,128]{1,0,2:T(4,128)(2,1)}, u32[]{:S(2)}, u32[]{:S(2)}) collective-permute-start(bf16[4,512,128]{1,0,2:T(4,128)(2,1)S(1)} %fusion.1), channel_id=1, source_target_pairs={{4,0},{8,4},{12,8},{16,12},{20,16},{24,20},{28,24},{32,28},{36,32}... | collective-permute-start | bytes 1572872 | tf_op jit(solution)/shard_map/ppermute | solution.py:64
  10.1 1.5 %rev.7 = bf16[512,128]{1,0:T(8,128)(2,1)} reverse(bf16[512,128]{1,0:T(8,128)(2,1)S(1)} %copy-done.5), dimensions={1} | reverse | bytes 262144 | tf_op jit(solution)/shard_map/rev | solution.py:68
  11.6 2.4 %collective-permute-done = bf16[4,512,128]{1,0,2:T(4,128)(2,1)} collective-permute-done((bf16[4,512,128]{1,0,2:T(4,128)(2,1)S(1)}, bf16[4,512,128]{1,0,2:T(4,128)(2,1)}, u32[]{:S(2)}, u32[]{:S(2)}) %collective-permute-start) | collective-permute-done | bytes 524320 | tf_op jit(solution)/shard_map/ppermute | solution.py:63
  14.0 1.2 %slice.50 = bf16[4,512,127]{1,0,2:T(4,128)(2,1)S(1)} slice(bf16[4,512,128]{1,0,2:T(4,128)(2,1)} %collective-permute-done), slice={[0:4], [0:512], [1:128]} | slice | bytes 1040384 | tf_op jit(solution)/shard_map/slice | solution.py:66
  15.2 23.5 %fusion.14 = f32[512,1,128]{0,1,2:T(1,128)S(1)} fusion(bf16[4,512,128]{1,0,2:T(4,128)(2,1)S(1)} %fusion.1, bf16[4,512,128]{1,0,2:T(4,128)(2,1)S(1)} %fusion.4, bf16[4,512,127]{1,0,2:T(4,128)(2,1)S(1)} %slice.50), kind=kOutput, calls=%fused_computation.32 | convolution fusion | flops 69197824 | bytes 1830912 | tf_op jit(solution)/shard_map/conv_general_dilated | solution.py:69
  39.0 1.9 %collective-permute-start.1 = (f32[64,4,128]{2,1,0:T(4,128)S(1)}, f32[64,4,128]{2,1,0:T(4,128)S(1)}, u32[]{:S(2)}, u32[]{:S(2)}) collective-permute-start(f32[64,4,128]{2,1,0:T(4,128)S(1)} %select_bitcast_fusion), channel_id=1, source_target_pairs={{0,4},{4,0},{1,5},{5,1},{2,6},{6,2},{3,7},{7,3},{8,12},{12,8},{9,1... | collective-permute-start | bytes 393224 | tf_op jit(solution)/shard_map/ppermute | solution.py:32
  40.9 1.6 %pad_maximum_fusion.1 = bf16[4,512,255]{1,0,2:T(4,128)(2,1)} fusion(bf16[4,512,128]{1,0,2:T(4,128)(2,1)S(1)} %fusion.4, bf16[4,512,127]{1,0,2:T(4,128)(2,1)S(1)} %slice.50), kind=kLoop, calls=%fused_computation.15 | loop fusion | flops 522240 | bytes 2088960 | tf_op jit(solution)/shard_map/concatenate | solution.py:66
  42.5 1.2 %slice.57 = bf16[4,512,127]{1,0,2:T(4,128)(2,1)S(1)} slice(bf16[4,512,128]{1,0,2:T(4,128)(2,1)} %collective-permute-done.4), slice={[0:4], [0:512], [0:127]} | slice | bytes 1040384 | tf_op jit(solution)/shard_map/slice | solution.py:67
  43.8 1.7 %pad_maximum_fusion.2 = bf16[4,512,255]{1,0,2:T(4,128)(2,1)} fusion(bf16[4,512,127]{1,0,2:T(4,128)(2,1)S(1)} %slice.57, bf16[4,512,128]{1,0,2:T(4,128)(2,1)S(1)} %fusion.1), kind=kLoop, calls=%fused_computation.16 | loop fusion | flops 522240 | bytes 2088960 | tf_op jit(solution)/shard_map/concatenate | solution.py:67
  45.7 4.3 %collective-permute-start.2 = (f32[32,4,128]{2,1,0:T(4,128)S(1)}, f32[32,4,128]{2,1,0:T(4,128)S(1)}, u32[]{:S(2)}, u32[]{:S(2)}) collective-permute-start(f32[32,4,128]{2,1,0:T(4,128)S(1)} %fusion.11), channel_id=1, source_target_pairs={{0,8},{8,0},{16,24},{24,16},{1,9},{9,1},{17,25},{25,17},{2,10},{10... | collective-permute-start | bytes 196616 | tf_op jit(solution)/shard_map/ppermute | solution.py:35
  50.0 10.4 %convolution_convert_fusion.1 = bf16[4,512,128]{1,0,2:T(4,128)(2,1)S(1)} fusion(bf16[4,512,255]{1,0,2:T(4,128)(2,1)S(1)} %copy-done.4, bf16[512,1,128]{0,1,2:T(2,128)(2,1)S(1)} %copy.37), kind=kOutput, calls=%fused_computation.8 | convolution fusion | flops 67371008 | bytes 1699840 | tf_op jit(solution)/shard_map/conv_general_dilated | solution.py:12
  60.6 2.6 %collective-permute-start.3 = (f32[16,4,128]{2,1,0:T(4,128)S(1)}, f32[16,4,128]{2,1,0:T(4,128)S(1)}, u32[]{:S(2)}, u32[]{:S(2)}) collective-permute-start(f32[16,4,128]{2,1,0:T(4,128)S(1)} %select_bitcast_fusion.1), channel_id=1, source_target_pairs={{0,16},{8,24},{16,0},{24,8},{1,17},{9,25},{17,1},{25,9},{2,18},{10... | collective-permute-start | bytes 98312 | tf_op jit(solution)/shard_map/ppermute | solution.py:32
  63.1 0.5 fusion.8
  63.7 1.2 %copy.45 = bf16[4,512,128]{2,1,0:T(8,128)(2,1)} copy(bf16[4,512,128]{1,0,2:T(4,128)(2,1)S(1)} %get-tuple-element.33) | data formatting | bytes 1048576
  64.9 3.0 %collective-permute-done.3 = f32[16,4,128]{2,1,0:T(4,128)S(1)} collective-permute-done((f32[16,4,128]{2,1,0:T(4,128)S(1)}, f32[16,4,128]{2,1,0:T(4,128)S(1)}, u32[]{:S(2)}, u32[]{:S(2)}) %collective-permute-start.3) | collective-permute-done | bytes 32800 | tf_op jit(solution)/shard_map/ppermute | solution.py:32
  67.9 0.6 fusion.13
  68.7 16.6 %all-to-all-start = ((f32[16,4,128]{2,1,0:T(4,128)}), f32[16,4,128]{2,1,0:T(4,128)S(1)}, u32[]{:S(2)}, u32[]{:S(2)}) async-start(f32[16,4,128]{2,1,0:T(4,128)} %fusion.13), calls=%async_computation | async-start | bytes 65536 | tf_op jit(solution)/shard_map/all_to_all | solution.py:85
  85.3 11.6 %convolution_convert_fusion = bf16[4,512,128]{1,0,2:T(4,128)(2,1)S(1)} fusion(bf16[4,512,255]{1,0,2:T(4,128)(2,1)} %pad_maximum_fusion.2, bf16[512,1,128]{0,1,2:T(2,128)(2,1)S(1)} %copy.44), kind=kOutput, calls=%fused_computation.7 | convolution fusion | flops 67371008 | bytes 1699840 | tf_op jit(solution)/shard_map/conv_general_dilated | solution.py:12
  97.0 1.0 all-to-all-done
  98.0 3.4 %collective-permute-start.5 = (f32[4,128]{1,0:T(4,128)S(1)}, f32[4,128]{1,0:T(4,128)S(1)}, u32[]{:S(2)}, u32[]{:S(2)}) collective-permute-start(f32[4,128]{1,0:T(4,128)S(1)} %reduce_sum.9), channel_id=1, source_target_pairs={{0,1},{1,0},{2,3},{3,2},{4,5},{5,4},{6,7},{7,6},{8,9},{9,8},{10,11... | collective-permute-start | bytes 6152 | tf_op jit(solution)/shard_map/ppermute | solution.py:45
  101.4 0.5 fusion.7
  101.9 1.6 %collective-permute-done.5 = f32[4,128]{1,0:T(4,128)S(1)} collective-permute-done((f32[4,128]{1,0:T(4,128)S(1)}, f32[4,128]{1,0:T(4,128)S(1)}, u32[]{:S(2)}, u32[]{:S(2)}) %collective-permute-start.5) | collective-permute-done | bytes 2080 | tf_op jit(solution)/shard_map/ppermute | solution.py:45
  103.5 4.9 %collective-permute-start.6 = (f32[4,128]{1,0:T(4,128)S(1)}, f32[4,128]{1,0:T(4,128)S(1)}, u32[]{:S(2)}, u32[]{:S(2)}) collective-permute-start(f32[4,128]{1,0:T(4,128)S(1)} %add.18), channel_id=1, source_target_pairs={{0,2},{1,3},{2,0},{3,1},{4,6},{5,7},{6,4},{7,5},{8,10},{9,11},{10,... | collective-permute-start | bytes 6152 | tf_op jit(solution)/shard_map/ppermute | solution.py:45
  108.4 1.3 %pad_maximum_fusion = bf16[3,4,512,128]{2,1,3,0:T(4,128)(2,1)S(1)} fusion(bf16[1,4,512,128]{2,1,3,0:T(4,128)(2,1)S(1)} %get-tuple-element.35, bf16[1,4,512,128]{2,1,3,0:T(4,128)(2,1)S(1)} %get-tuple-element.34, bf16[1,4,512,128]{2,1,3,0:T(4,128)(2,1)S(1)} %get-tuple-element.32), kind=kLoop, calls=%fused_computation | loop fusion | flops 1572864 | bytes 3145728 | tf_op jit(solution)/shard_map/stack | solution.py:92
  109.7 2.5 %copy.46 = bf16[3,4,512,128]{3,2,1,0:T(8,128)(2,1)} copy(bf16[3,4,512,128]{2,1,3,0:T(4,128)(2,1)S(1)} %pad_maximum_fusion) | data formatting | bytes 3145728
  112.2 0.6 add_multiply_fusion
  (33 shorter events, 1.4 us)
Async XLA Ops:
  2.5 3.2 %copy-start = (bf16[1,4,512,128]{2,1,3,0:T(4,128)(2,1)}, bf16[1,4,512,128]{2,1,3,0:T(4,128)(2,1)S(1)}, u32[]{:S(2)}) copy-start(bf16[1,4,512,128]{2,1,3,0:T(4,128)(2,1)S(1)} %copy.48) | copy-start | bytes 1572868
  2.9 3.2 %copy-start.2 = (bf16[1,4,512,128]{2,1,3,0:T(4,128)(2,1)}, bf16[1,4,512,128]{2,1,3,0:T(4,128)(2,1)S(1)}, u32[]{:S(2)}) copy-start(bf16[1,4,512,128]{2,1,3,0:T(4,128)(2,1)S(1)} %copy.49) | copy-start | bytes 1572868
  2.9 2.8 %copy-start.7 = (bf16[4,512,128]{2,1,0:T(8,128)(2,1)S(1)}, bf16[4,512,128]{2,1,0:T(8,128)(2,1)}, u32[]{:S(2)}) copy-start(bf16[4,512,128]{2,1,0:T(8,128)(2,1)} %param.5) | copy-start | bytes 1572868
  3.2 10.7 %collective-permute-start = (bf16[4,512,128]{1,0,2:T(4,128)(2,1)S(1)}, bf16[4,512,128]{1,0,2:T(4,128)(2,1)}, u32[]{:S(2)}, u32[]{:S(2)}) collective-permute-start(bf16[4,512,128]{1,0,2:T(4,128)(2,1)S(1)} %fusion.4), channel_id=1, source_target_pairs={{0,4},{4,8},{8,12},{12,16},{16,20},{20,24},{24,28},{28,32},{32,36}... | collective-permute-start | bytes 1572872 | tf_op jit(solution)/shard_map/ppermute | solution.py:63
  5.7 4.4 %copy-start.5 = (bf16[512,128]{1,0:T(8,128)(2,1)S(1)}, bf16[512,128]{1,0:T(8,128)(2,1)}, u32[]{:S(2)}) copy-start(bf16[512,128]{1,0:T(8,128)(2,1)} %param.4) | copy-start | bytes 393220
  6.4 36.1 %collective-permute-start.4 = (bf16[4,512,128]{1,0,2:T(4,128)(2,1)S(1)}, bf16[4,512,128]{1,0,2:T(4,128)(2,1)}, u32[]{:S(2)}, u32[]{:S(2)}) collective-permute-start(bf16[4,512,128]{1,0,2:T(4,128)(2,1)S(1)} %fusion.1), channel_id=1, source_target_pairs={{4,0},{8,4},{12,8},{16,12},{20,16},{24,20},{28,24},{32,28},{36,32}... | collective-permute-start | bytes 1572872 | tf_op jit(solution)/shard_map/ppermute | solution.py:64
  39.0 6.5 %collective-permute-start.1 = (f32[64,4,128]{2,1,0:T(4,128)S(1)}, f32[64,4,128]{2,1,0:T(4,128)S(1)}, u32[]{:S(2)}, u32[]{:S(2)}) collective-permute-start(f32[64,4,128]{2,1,0:T(4,128)S(1)} %select_bitcast_fusion), channel_id=1, source_target_pairs={{0,4},{4,0},{1,5},{5,1},{2,6},{6,2},{3,7},{7,3},{8,12},{12,8},{9,1... | collective-permute-start | bytes 393224 | tf_op jit(solution)/shard_map/ppermute | solution.py:32
  43.8 1.8 %copy-start.6 = (bf16[512,128]{1,0:T(8,128)(2,1)S(1)}, bf16[512,128]{1,0:T(8,128)(2,1)}, u32[]{:S(2)}) copy-start(bf16[512,128]{1,0:T(8,128)(2,1)} %rev.7) | copy-start | bytes 393220
  43.8 6.3 %copy-start.4 = (bf16[4,512,255]{1,0,2:T(4,128)(2,1)S(1)}, bf16[4,512,255]{1,0,2:T(4,128)(2,1)}, u32[]{:S(2)}) copy-start(bf16[4,512,255]{1,0,2:T(4,128)(2,1)} %pad_maximum_fusion.1) | copy-start | bytes 3133444
  45.7 14.8 %collective-permute-start.2 = (f32[32,4,128]{2,1,0:T(4,128)S(1)}, f32[32,4,128]{2,1,0:T(4,128)S(1)}, u32[]{:S(2)}, u32[]{:S(2)}) collective-permute-start(f32[32,4,128]{2,1,0:T(4,128)S(1)} %fusion.11), channel_id=1, source_target_pairs={{0,8},{8,0},{16,24},{24,16},{1,9},{9,1},{17,25},{25,17},{2,10},{10... | collective-permute-start | bytes 196616 | tf_op jit(solution)/shard_map/ppermute | solution.py:35
  60.6 7.3 %collective-permute-start.3 = (f32[16,4,128]{2,1,0:T(4,128)S(1)}, f32[16,4,128]{2,1,0:T(4,128)S(1)}, u32[]{:S(2)}, u32[]{:S(2)}) collective-permute-start(f32[16,4,128]{2,1,0:T(4,128)S(1)} %select_bitcast_fusion.1), channel_id=1, source_target_pairs={{0,16},{8,24},{16,0},{24,8},{1,17},{9,25},{17,1},{25,9},{2,18},{10... | collective-permute-start | bytes 98312 | tf_op jit(solution)/shard_map/ppermute | solution.py:32
  68.7 29.3 %all-to-all-start = ((f32[16,4,128]{2,1,0:T(4,128)}), f32[16,4,128]{2,1,0:T(4,128)S(1)}, u32[]{:S(2)}, u32[]{:S(2)}) async-start(f32[16,4,128]{2,1,0:T(4,128)} %fusion.13), calls=%async_computation | async-start | bytes 65536 | tf_op jit(solution)/shard_map/all_to_all | solution.py:85
  85.3 16.1 %copy-start.1 = (bf16[1,4,512,128]{2,1,3,0:T(4,128)(2,1)S(1)}, bf16[1,4,512,128]{2,1,3,0:T(4,128)(2,1)}, u32[]{:S(2)}) copy-start(bf16[1,4,512,128]{2,1,3,0:T(4,128)(2,1)} %copy-done) | copy-start | bytes 1572868
  85.3 16.1 %copy-start.3 = (bf16[1,4,512,128]{2,1,3,0:T(4,128)(2,1)S(1)}, bf16[1,4,512,128]{2,1,3,0:T(4,128)(2,1)}, u32[]{:S(2)}) copy-start(bf16[1,4,512,128]{2,1,3,0:T(4,128)(2,1)} %copy-done.2) | copy-start | bytes 1572868
  98.0 5.5 %collective-permute-start.5 = (f32[4,128]{1,0:T(4,128)S(1)}, f32[4,128]{1,0:T(4,128)S(1)}, u32[]{:S(2)}, u32[]{:S(2)}) collective-permute-start(f32[4,128]{1,0:T(4,128)S(1)} %reduce_sum.9), channel_id=1, source_target_pairs={{0,1},{1,0},{2,3},{3,2},{4,5},{5,4},{6,7},{7,6},{8,9},{9,8},{10,11... | collective-permute-start | bytes 6152 | tf_op jit(solution)/shard_map/ppermute | solution.py:45
  103.5 8.7 %collective-permute-start.6 = (f32[4,128]{1,0:T(4,128)S(1)}, f32[4,128]{1,0:T(4,128)S(1)}, u32[]{:S(2)}, u32[]{:S(2)}) collective-permute-start(f32[4,128]{1,0:T(4,128)S(1)} %add.18), channel_id=1, source_target_pairs={{0,2},{1,3},{2,0},{3,1},{4,6},{5,7},{6,4},{7,5},{8,10},{9,11},{10,... | collective-permute-start | bytes 6152 | tf_op jit(solution)/shard_map/ppermute | solution.py:45

commit v2 on v1

--- a/solution.py
+++ b/solution.py
@@ -61,10 +61,8 @@
         jnp.bfloat16
     )
     earlier = lax.ppermute(gated, CONTEXT, [(i, i + 1) for i in range(blocks - 1)])
-    later = lax.ppermute(grad_filtered, CONTEXT, [(i + 1, i) for i in range(blocks - 1)])
     halo = filter_taps - 1
     gated_ext = jnp.concatenate([earlier[:, :, local_tokens - halo:], gated], 2)
-    grad_ext = jnp.concatenate([grad_filtered, later[:, :, :halo]], 2)
     reversed_taps = long_filter[:, ::-1][:, None, :]
     tap_sums = lax.conv_general_dilated(
         gated_ext,
@@ -76,6 +74,9 @@
         preferred_element_type=jnp.float32,
     )
     partial_taps = tap_sums[:, 0, ::-1]
+    sent, partial_taps = lax.optimization_barrier((grad_filtered, partial_taps))
+    later = lax.ppermute(sent, CONTEXT, [(i + 1, i) for i in range(blocks - 1)])
+    grad_ext = jnp.concatenate([grad_filtered, later[:, :, :halo]], 2)
     rows = partial_taps.reshape(blocks, groups // blocks, filter_taps)
     forward = lambda lhs, rhs: grouped_conv(lhs, rhs, groups).astype(jnp.bfloat16)
     rows = halving_step(rows, "core", 0)

time: 113 us -> 116 us (1.027)
  the two profiles are of different devices: /device:TPU:8 before, /device:TPU:2 now
where the time goes in v2:
time: 116 us
  starting transfers between devices  47.5 us (41%)
  matrix products  45.5 us (39%)
  local copies, waits for them, and re-layouts  10.1 us (9%)
  other arithmetic  6.59 us (6%)
  waiting for transfers between devices  4.87 us (4%)
    conv_general_dilated x1, matrix products, body(): lax.conv_general_dilated(gated_ext, grad_filtered, window_strides=(1,), p...  23.5 us
    conv_general_dilated x2, matrix products, grouped_conv(): lax.conv_general_dilated(lhs, rhs, window_strides=(1,), padding='VALID',...  22 us
    all_to_all x1, starting transfers between devices, body(): rows = lax.all_to_all(rows, 'z', split_axis=0, concat_axis=0, tiled=True)  18.9 us
    ppermute x2, starting transfers between devices, halving_step(): return keep + lax.ppermute(give, axis, pairs)  13.1 us
    ppermute x2, starting transfers between devices, butterfly_sum(): values = values + lax.ppermute(values, axis, pairs)  6.46 us
    unnamed x19, local copies, waits for them, and re-layouts  5.29 us
    ppermute x1, starting transfers between devices, halving_step(): received = lax.ppermute(give, axis, pairs)  5.02 us
    ppermute x1, starting transfers between devices, body(): lax.ppermute(gated, CONTEXT, [(i, i + 1) for i in range(blocks - 1)])  2.71 us
  transfers between devices with their start and end apart: 8, of which 3 were waited for; matrix products, arithmetic and copies ran while one was open for 28% of the time, Pallas kernels for 0%

profile of v2, /device:TPU:2, one launch (start us, length us, event | category | flops | bytes accessed | tf_op | source)
XLA Modules:
  0.0 115.5 jit_solution(14558232867683154228)
XLA Ops:
  0.6 1.5 %fusion.15 = (bf16[1,4,512,128]{3,2,1,0:T(8,128)(2,1)S(1)}, bf16[1,4,512,128]{3,2,1,0:T(8,128)(2,1)S(1)}, bf16[1,4,512,128]{3,2,1,0:T(8,128)(2,1)S(1)}) fusion(bf16[3,4,512,128]{3,2,1,0:T(8,128)(2,1)} %param.3), kind=kLoop, calls=%fused_computation.34 | loop fusion | bytes 3145728 | tf_op jit(solution)/shard_map/slice | solution.py:54
  2.1 0.4 copy.48
  2.5 0.4 copy.49
  2.9 0.3 fusion.4
  3.2 2.7 %collective-permute-start = (bf16[4,512,128]{1,0,2:T(4,128)(2,1)S(1)}, bf16[4,512,128]{1,0,2:T(4,128)(2,1)}, u32[]{:S(2)}, u32[]{:S(2)}) collective-permute-start(bf16[4,512,128]{1,0,2:T(4,128)(2,1)S(1)} %fusion.4), channel_id=1, source_target_pairs={{0,4},{4,8},{8,12},{12,16},{16,20},{20,24},{24,28},{28,32},{32,36}... | collective-permute-start | bytes 1572872 | tf_op jit(solution)/shard_map/ppermute | solution.py:63
  5.9 0.4 copy.50
  6.4 0.4 copy.27
  6.8 0.4 rev.7
  7.2 0.3 fusion.1
  7.5 1.2 %slice.50 = bf16[4,512,127]{1,0,2:T(4,128)(2,1)S(1)} slice(bf16[4,512,128]{1,0,2:T(4,128)(2,1)} %collective-permute-done), slice={[0:4], [0:512], [1:128]} | slice | bytes 1040384 | tf_op jit(solution)/shard_map/slice | solution.py:65
  8.7 23.5 %fusion.14 = f32[512,1,128]{0,1,2:T(1,128)S(1)} fusion(bf16[4,512,128]{1,0,2:T(4,128)(2,1)S(1)} %fusion.1, bf16[4,512,128]{1,0,2:T(4,128)(2,1)S(1)} %fusion.4, bf16[4,512,127]{1,0,2:T(4,128)(2,1)S(1)} %slice.50), kind=kOutput, calls=%fused_computation.33 | convolution fusion | flops 69197824 | bytes 1830912 | tf_op jit(solution)/shard_map/conv_general_dilated | solution.py:67
  32.4 7.5 %collective-permute-start.1 = (f32[64,4,128]{2,1,0:T(4,128)S(1)}, f32[64,4,128]{2,1,0:T(4,128)S(1)}, u32[]{:S(2)}, u32[]{:S(2)}) collective-permute-start(f32[64,4,128]{2,1,0:T(4,128)S(1)} %select_bitcast_fusion), channel_id=1, source_target_pairs={{0,4},{4,0},{1,5},{5,1},{2,6},{6,2},{3,7},{7,3},{8,12},{12,8},{9,1... | collective-permute-start | bytes 393224 | tf_op jit(solution)/shard_map/ppermute | solution.py:32
  39.9 1.3 %collective-permute-start.4 = (bf16[4,512,128]{1,0,2:T(4,128)(2,1)S(1)}, bf16[4,512,128]{1,0,2:T(4,128)(2,1)}, u32[]{:S(2)}, u32[]{:S(2)}) collective-permute-start(bf16[4,512,128]{1,0,2:T(4,128)(2,1)S(1)} %fusion.1), channel_id=1, source_target_pairs={{4,0},{8,4},{12,8},{16,12},{20,16},{24,20},{28,24},{32,28},{36,32}... | collective-permute-start | bytes 1572872 | tf_op jit(solution)/shard_map/ppermute | solution.py:78
  41.2 1.6 %pad_maximum_fusion.1 = bf16[4,512,255]{1,0,2:T(4,128)(2,1)} fusion(bf16[4,512,128]{1,0,2:T(4,128)(2,1)S(1)} %fusion.4, bf16[4,512,127]{1,0,2:T(4,128)(2,1)S(1)} %slice.50), kind=kLoop, calls=%fused_computation.15 | loop fusion | flops 522240 | bytes 2088960 | tf_op jit(solution)/shard_map/concatenate | solution.py:65
  43.2 5.0 %collective-permute-start.2 = (f32[32,4,128]{2,1,0:T(4,128)S(1)}, f32[32,4,128]{2,1,0:T(4,128)S(1)}, u32[]{:S(2)}, u32[]{:S(2)}) collective-permute-start(f32[32,4,128]{2,1,0:T(4,128)S(1)} %fusion.11), channel_id=1, source_target_pairs={{0,8},{8,0},{16,24},{24,16},{1,9},{9,1},{17,25},{25,17},{2,10},{10... | collective-permute-start | bytes 196616 | tf_op jit(solution)/shard_map/ppermute | solution.py:35
  48.2 11.6 %convolution_convert_fusion.1 = bf16[4,512,128]{1,0,2:T(4,128)(2,1)S(1)} fusion(bf16[4,512,255]{1,0,2:T(4,128)(2,1)} %pad_maximum_fusion.1, bf16[512,1,128]{0,1,2:T(2,128)(2,1)S(1)} %copy.37), kind=kOutput, calls=%fused_computation.8 | convolution fusion | flops 67371008 | bytes 1699840 | tf_op jit(solution)/shard_map/conv_general_dilated | solution.py:12
  59.8 5.6 %collective-permute-start.3 = (f32[16,4,128]{2,1,0:T(4,128)S(1)}, f32[16,4,128]{2,1,0:T(4,128)S(1)}, u32[]{:S(2)}, u32[]{:S(2)}) collective-permute-start(f32[16,4,128]{2,1,0:T(4,128)S(1)} %select_bitcast_fusion.1), channel_id=1, source_target_pairs={{0,16},{8,24},{16,0},{24,8},{1,17},{9,25},{17,1},{25,9},{2,18},{10... | collective-permute-start | bytes 98312 | tf_op jit(solution)/shard_map/ppermute | solution.py:32
  65.5 0.5 fusion.8
  66.0 1.2 %copy.45 = bf16[4,512,128]{2,1,0:T(8,128)(2,1)} copy(bf16[4,512,128]{1,0,2:T(4,128)(2,1)S(1)} %get-tuple-element.37) | data formatting | bytes 1048576
  67.3 0.6 fusion.13
  68.0 1.2 %slice.57 = bf16[4,512,127]{1,0,2:T(4,128)(2,1)S(1)} slice(bf16[4,512,128]{1,0,2:T(4,128)(2,1)} %collective-permute-done.4), slice={[0:4], [0:512], [0:127]} | slice | bytes 1040384 | tf_op jit(solution)/shard_map/slice | solution.py:79
  69.2 0.7 pad_maximum_fusion.2
  70.1 18.9 %all-to-all-start = ((f32[16,4,128]{2,1,0:T(4,128)}), f32[16,4,128]{2,1,0:T(4,128)S(1)}, u32[]{:S(2)}, u32[]{:S(2)}) async-start(f32[16,4,128]{2,1,0:T(4,128)} %fusion.13), calls=%async_computation | async-start | bytes 65536 | tf_op jit(solution)/shard_map/all_to_all | solution.py:86
  89.0 10.4 %convolution_convert_fusion = bf16[4,512,128]{1,0,2:T(4,128)(2,1)S(1)} fusion(bf16[4,512,255]{1,0,2:T(4,128)(2,1)S(1)} %pad_maximum_fusion.2, bf16[512,1,128]{0,1,2:T(2,128)(2,1)S(1)} %copy.44), kind=kOutput, calls=%fused_computation.7 | convolution fusion | flops 67371008 | bytes 1699840 | tf_op jit(solution)/shard_map/conv_general_dilated | solution.py:12
  99.4 2.2 %all-to-all-done = f32[16,4,128]{2,1,0:T(4,128)S(1)} async-done(((f32[16,4,128]{2,1,0:T(4,128)}), f32[16,4,128]{2,1,0:T(4,128)S(1)}, u32[]{:S(2)}, u32[]{:S(2)}) %all-to-all-start) | async-done | bytes 32800 | tf_op jit(solution)/shard_map/all_to_all | solution.py:86
  101.6 2.4 %collective-permute-start.5 = (f32[4,128]{1,0:T(4,128)S(1)}, f32[4,128]{1,0:T(4,128)S(1)}, u32[]{:S(2)}, u32[]{:S(2)}) collective-permute-start(f32[4,128]{1,0:T(4,128)S(1)} %reduce_sum.9), channel_id=1, source_target_pairs={{0,1},{1,0},{2,3},{3,2},{4,5},{5,4},{6,7},{7,6},{8,9},{9,8},{10,11... | collective-permute-start | bytes 6152 | tf_op jit(solution)/shard_map/ppermute | solution.py:45
  104.1 0.5 fusion.7
  104.6 2.5 %collective-permute-done.5 = f32[4,128]{1,0:T(4,128)S(1)} collective-permute-done((f32[4,128]{1,0:T(4,128)S(1)}, f32[4,128]{1,0:T(4,128)S(1)}, u32[]{:S(2)}, u32[]{:S(2)}) %collective-permute-start.5) | collective-permute-done | bytes 2080 | tf_op jit(solution)/shard_map/ppermute | solution.py:45
  107.1 4.0 %collective-permute-start.6 = (f32[4,128]{1,0:T(4,128)S(1)}, f32[4,128]{1,0:T(4,128)S(1)}, u32[]{:S(2)}, u32[]{:S(2)}) collective-permute-start(f32[4,128]{1,0:T(4,128)S(1)} %add.18), channel_id=1, source_target_pairs={{0,2},{1,3},{2,0},{3,1},{4,6},{5,7},{6,4},{7,5},{8,10},{9,11},{10,... | collective-permute-start | bytes 6152 | tf_op jit(solution)/shard_map/ppermute | solution.py:45
  111.1 1.3 %pad_maximum_fusion = bf16[3,4,512,128]{2,1,3,0:T(4,128)(2,1)S(1)} fusion(bf16[1,4,512,128]{2,1,3,0:T(4,128)(2,1)S(1)} %get-tuple-element.39, bf16[1,4,512,128]{2,1,3,0:T(4,128)(2,1)S(1)} %get-tuple-element.38, bf16[1,4,512,128]{2,1,3,0:T(4,128)(2,1)S(1)} %get-tuple-element.36), kind=kLoop, calls=%fused_computation | loop fusion | flops 1572864 | bytes 3145728 | tf_op jit(solution)/shard_map/stack | solution.py:93
  112.4 2.5 %copy.46 = bf16[3,4,512,128]{3,2,1,0:T(8,128)(2,1)} copy(bf16[3,4,512,128]{2,1,3,0:T(4,128)(2,1)S(1)} %pad_maximum_fusion) | data formatting | bytes 3145728
  114.9 0.6 add_multiply_fusion
  (30 shorter events, 0.9 us)
Async XLA Ops:
  2.5 3.8 %copy-start = (bf16[1,4,512,128]{2,1,3,0:T(4,128)(2,1)}, bf16[1,4,512,128]{2,1,3,0:T(4,128)(2,1)S(1)}, u32[]{:S(2)}) copy-start(bf16[1,4,512,128]{2,1,3,0:T(4,128)(2,1)S(1)} %copy.48) | copy-start | bytes 1572868
  2.9 3.9 %copy-start.2 = (bf16[1,4,512,128]{2,1,3,0:T(4,128)(2,1)}, bf16[1,4,512,128]{2,1,3,0:T(4,128)(2,1)S(1)}, u32[]{:S(2)}) copy-start(bf16[1,4,512,128]{2,1,3,0:T(4,128)(2,1)S(1)} %copy.49) | copy-start | bytes 1572868
  2.9 3.4 %copy-start.5 = (bf16[4,512,128]{2,1,0:T(8,128)(2,1)S(1)}, bf16[4,512,128]{2,1,0:T(8,128)(2,1)}, u32[]{:S(2)}) copy-start(bf16[4,512,128]{2,1,0:T(8,128)(2,1)} %param.5) | copy-start | bytes 1572868
  2.9 3.9 %copy-start.4 = (bf16[512,128]{1,0:T(8,128)(2,1)S(1)}, bf16[512,128]{1,0:T(8,128)(2,1)}, u32[]{:S(2)}) copy-start(bf16[512,128]{1,0:T(8,128)(2,1)} %param.4) | copy-start | bytes 393220
  3.2 4.3 %collective-permute-start = (bf16[4,512,128]{1,0,2:T(4,128)(2,1)S(1)}, bf16[4,512,128]{1,0,2:T(4,128)(2,1)}, u32[]{:S(2)}, u32[]{:S(2)}) collective-permute-start(bf16[4,512,128]{1,0,2:T(4,128)(2,1)S(1)} %fusion.4), channel_id=1, source_target_pairs={{0,4},{4,8},{8,12},{12,16},{16,20},{20,24},{24,28},{28,32},{32,36}... | collective-permute-start | bytes 1572872 | tf_op jit(solution)/shard_map/ppermute | solution.py:63
  32.4 10.4 %collective-permute-start.1 = (f32[64,4,128]{2,1,0:T(4,128)S(1)}, f32[64,4,128]{2,1,0:T(4,128)S(1)}, u32[]{:S(2)}, u32[]{:S(2)}) collective-permute-start(f32[64,4,128]{2,1,0:T(4,128)S(1)} %select_bitcast_fusion), channel_id=1, source_target_pairs={{0,4},{4,0},{1,5},{5,1},{2,6},{6,2},{3,7},{7,3},{8,12},{12,8},{9,1... | collective-permute-start | bytes 393224 | tf_op jit(solution)/shard_map/ppermute | solution.py:32
  39.9 28.0 %collective-permute-start.4 = (bf16[4,512,128]{1,0,2:T(4,128)(2,1)S(1)}, bf16[4,512,128]{1,0,2:T(4,128)(2,1)}, u32[]{:S(2)}, u32[]{:S(2)}) collective-permute-start(bf16[4,512,128]{1,0,2:T(4,128)(2,1)S(1)} %fusion.1), channel_id=1, source_target_pairs={{4,0},{8,4},{12,8},{16,12},{20,16},{24,20},{28,24},{32,28},{36,32}... | collective-permute-start | bytes 1572872 | tf_op jit(solution)/shard_map/ppermute | solution.py:78
  43.2 16.6 %collective-permute-start.2 = (f32[32,4,128]{2,1,0:T(4,128)S(1)}, f32[32,4,128]{2,1,0:T(4,128)S(1)}, u32[]{:S(2)}, u32[]{:S(2)}) collective-permute-start(f32[32,4,128]{2,1,0:T(4,128)S(1)} %fusion.11), channel_id=1, source_target_pairs={{0,8},{8,0},{16,24},{24,16},{1,9},{9,1},{17,25},{25,17},{2,10},{10... | collective-permute-start | bytes 196616 | tf_op jit(solution)/shard_map/ppermute | solution.py:35
  59.8 7.5 %collective-permute-start.3 = (f32[16,4,128]{2,1,0:T(4,128)S(1)}, f32[16,4,128]{2,1,0:T(4,128)S(1)}, u32[]{:S(2)}, u32[]{:S(2)}) collective-permute-start(f32[16,4,128]{2,1,0:T(4,128)S(1)} %select_bitcast_fusion.1), channel_id=1, source_target_pairs={{0,16},{8,24},{16,0},{24,8},{1,17},{9,25},{17,1},{25,9},{2,18},{10... | collective-permute-start | bytes 98312 | tf_op jit(solution)/shard_map/ppermute | solution.py:32
  70.1 31.5 %all-to-all-start = ((f32[16,4,128]{2,1,0:T(4,128)}), f32[16,4,128]{2,1,0:T(4,128)S(1)}, u32[]{:S(2)}, u32[]{:S(2)}) async-start(f32[16,4,128]{2,1,0:T(4,128)} %fusion.13), calls=%async_computation | async-start | bytes 65536 | tf_op jit(solution)/shard_map/all_to_all | solution.py:86
  88.9 15.1 %copy-start.1 = (bf16[1,4,512,128]{2,1,3,0:T(4,128)(2,1)S(1)}, bf16[1,4,512,128]{2,1,3,0:T(4,128)(2,1)}, u32[]{:S(2)}) copy-start(bf16[1,4,512,128]{2,1,3,0:T(4,128)(2,1)} %copy-done) | copy-start | bytes 1572868
  88.9 15.1 %copy-start.3 = (bf16[1,4,512,128]{2,1,3,0:T(4,128)(2,1)S(1)}, bf16[1,4,512,128]{2,1,3,0:T(4,128)(2,1)}, u32[]{:S(2)}) copy-start(bf16[1,4,512,128]{2,1,3,0:T(4,128)(2,1)} %copy-done.2) | copy-start | bytes 1572868
  101.6 5.5 %collective-permute-start.5 = (f32[4,128]{1,0:T(4,128)S(1)}, f32[4,128]{1,0:T(4,128)S(1)}, u32[]{:S(2)}, u32[]{:S(2)}) collective-permute-start(f32[4,128]{1,0:T(4,128)S(1)} %reduce_sum.9), channel_id=1, source_target_pairs={{0,1},{1,0},{2,3},{3,2},{4,5},{5,4},{6,7},{7,6},{8,9},{9,8},{10,11... | collective-permute-start | bytes 6152 | tf_op jit(solution)/shard_map/ppermute | solution.py:45
  107.1 7.8 %collective-permute-start.6 = (f32[4,128]{1,0:T(4,128)S(1)}, f32[4,128]{1,0:T(4,128)S(1)}, u32[]{:S(2)}, u32[]{:S(2)}) collective-permute-start(f32[4,128]{1,0:T(4,128)S(1)} %add.18), channel_id=1, source_target_pairs={{0,2},{1,3},{2,0},{3,1},{4,6},{5,7},{6,4},{7,5},{8,10},{9,11},{10,... | collective-permute-start | bytes 6152 | tf_op jit(solution)/shard_map/ppermute | solution.py:45
